TPU v7x, 32 devices: a whole 2x2x4 slice. The times are simulated.
32 devices in a mesh: fsdp: 8 (over y, x, core), dp: 4 (over z).
Axes of the slice: x: 2, y: 2, z: 4, core: 2. Of those that a mesh axis runs over, the one named last changes fastest.
Arguments:
- tokens: bfloat16 [131072, 1024], P(('fsdp', 'dp')), may hold values from -6 to 6
- cotangent: bfloat16 [131072, 1024], P(('fsdp', 'dp')), may hold values from -6 to 6
- lengths: int32 [256], P(('fsdp', 'dp')), may hold values from 8 to 2048, as said below
- selected: int32 [16384], P(('fsdp', 'dp')), may hold values from 0 to 4095, as said below
- attn_in: bfloat16 [1024, 3072], P('fsdp'), may hold values from -0.1875 to 0.1875
- attn_out: bfloat16 [1024, 1024], P('fsdp'), may hold values from -0.75 to 0.75
- mlp_in: bfloat16 [1024, 4096], P('fsdp'), may hold values from -0.1875 to 0.1875
- mlp_out: bfloat16 [4096, 1024], P('fsdp'), may hold values from -0.09375 to 0.09375
- norm_attn: bfloat16 [1024], P('fsdp'), may hold values from 0.5 to 1.5
- norm_mlp: bfloat16 [1024], P('fsdp'), may hold values from 0.5 to 1.5
- router: bfloat16 [1024], replicated, may hold values from -0.1875 to 0.1875
Outputs:
- output: bfloat16 [131072, 1024], P(('fsdp', 'dp'))
- grad_tokens: bfloat16 [131072, 1024], P(('fsdp', 'dp'))
- grad_attn_in: float32 [1024, 3072], P('fsdp')
- grad_attn_out: float32 [1024, 1024], P('fsdp')
- grad_mlp_in: float32 [1024, 4096], P('fsdp')
- grad_mlp_out: float32 [4096, 1024], P('fsdp')
- grad_norm_attn: float32 [1024], P('fsdp')
- grad_norm_mlp: float32 [1024], P('fsdp')
- grad_router: float32 [1024], replicated
Inputs may be any that keep to these rules, and one draw needn't show every extreme that they name: `lengths`: each aligned block of 8 entries (one device's sequences, in order) holds multiples of 8 that sum to 4096; exactly one of them equals 2048. `selected`: each aligned block of 512 entries lists distinct positions within its device's 4096 tokens in ascending order; a sequence of length L has exactly L / 8 of its positions listed.
All inputs are finite; a program needn't handle non-finite values.
Results may differ from a plain program's by a relative error of at most 0.014.
Values may be sent and summed in bfloat16 or wider, within the bound.
No kernel may reach another device: no remote copies, remote signals or barrier semaphores. Data moves between devices by JAX's collectives and lax.ppermute only.
A program may use at most 192 MiB of HBM per device.

v0:
```python
import jax
import jax.numpy as jnp
from jax import lax
from jax.sharding import PartitionSpec as P

HEADS = 16
HEAD = 64
EPS = 1e-06
MASKED = -1e30


def rms_scale(values, gain_vec):
    return values * lax.rsqrt(jnp.mean(values * values, axis=-1, keepdims=True) + EPS) * gain_vec


def seq_mask(lengths, selected):
    seq_ends = jnp.cumsum(lengths)
    owner_seq = jnp.sum((selected[:, None] >= seq_ends[None, :]).astype(jnp.int32), axis=1)
    return (owner_seq[:, None] == owner_seq[None, :]) & (selected[None, :] <= selected[:, None])


def split_heads(matrix):
    return matrix.reshape(matrix.shape[0], HEADS, HEAD)


def masked_scores(query_heads, key_heads, allowed, score_scale):
    scores = (
        jnp.einsum("qhd,khd->hqk", query_heads, key_heads, preferred_element_type=jnp.float32)
        * score_scale
    )
    return jnp.where(allowed[None], scores, MASKED)


def per_device(
    tokens,
    cotangent,
    lengths,
    selected,
    attn_in,
    attn_out,
    mlp_in,
    mlp_out,
    norm_attn,
    norm_mlp,
    router,
):
    model_width = tokens.shape[1]
    row_count = selected.shape[0]
    score_scale = HEAD ** (-0.5)
    w_qkv, w_out, gain_attn, gain_mlp = (
        lax.all_gather(attn_in, "fsdp", axis=0, tiled=True),
        lax.all_gather(attn_out, "fsdp", axis=0, tiled=True),
        lax.all_gather(norm_attn, "fsdp", axis=0, tiled=True),
        lax.all_gather(norm_mlp, "fsdp", axis=0, tiled=True),
    )
    w_in, w_down = (
        lax.all_gather(mlp_in, "fsdp", axis=0, tiled=True),
        lax.all_gather(mlp_out, "fsdp", axis=0, tiled=True),
    )
    gain_one = gain_attn.astype(jnp.float32)
    gain_two = gain_mlp.astype(jnp.float32)
    positions = lax.broadcasted_iota(jnp.int32, (row_count, tokens.shape[0]), 1)
    select = (selected[:, None] == positions).astype(jnp.bfloat16)
    routed = jnp.dot(select, tokens, preferred_element_type=jnp.float32)
    routed_low = routed.astype(jnp.bfloat16)
    router_rate = jnp.dot(routed_low, router, preferred_element_type=jnp.float32)
    allowed = seq_mask(lengths, selected)
    normed_float, norm_pull = jax.vjp(rms_scale, routed, gain_one)
    normed = normed_float.astype(jnp.bfloat16)
    qkv = jnp.dot(normed, w_qkv, preferred_element_type=jnp.float32).astype(jnp.bfloat16)
    query_heads = split_heads(qkv[:, :model_width])
    key_heads = split_heads(qkv[:, model_width : 2 * model_width])
    value_heads = split_heads(qkv[:, 2 * model_width :])
    scores = masked_scores(query_heads, key_heads, allowed, score_scale)
    highest = jnp.max(scores, axis=-1, keepdims=True)
    exponent = jnp.exp(scores - highest)
    row_total = jnp.sum(exponent, axis=-1, keepdims=True)
    probabilities = (exponent / row_total).astype(jnp.bfloat16)
    log_total = highest + jnp.log(row_total)
    attn_mix = jnp.einsum(
        "hqk,khd->qhd", probabilities, value_heads, preferred_element_type=jnp.float32
    )
    attn_mix = attn_mix.reshape(row_count, model_width).astype(jnp.bfloat16)
    attended = jnp.dot(attn_mix, w_out, preferred_element_type=jnp.float32)
    middle = routed + attended
    normed_two_float, middle_pull = jax.vjp(rms_scale, middle, gain_two)
    normed_two = normed_two_float.astype(jnp.bfloat16)
    pre_gelu = jnp.dot(normed_two, w_in, preferred_element_type=jnp.float32)
    active_float, gelu_pull = jax.vjp(jax.nn.gelu, pre_gelu)
    active = active_float.astype(jnp.bfloat16)
    expanded = jnp.dot(active, w_down, preferred_element_type=jnp.float32)
    update = attended + expanded
    branch = (router_rate[:, None] * update).astype(jnp.bfloat16)
    output = (
        tokens.astype(jnp.float32)
        + jnp.einsum("kt,kd->td", select, branch, preferred_element_type=jnp.float32)
    ).astype(jnp.bfloat16)
    w_qkv_back, w_out_back = (
        lax.all_gather(attn_in, "fsdp", axis=0, tiled=True),
        lax.all_gather(attn_out, "fsdp", axis=0, tiled=True),
    )
    w_in_back, w_down_back = (
        lax.all_gather(mlp_in, "fsdp", axis=0, tiled=True),
        lax.all_gather(mlp_out, "fsdp", axis=0, tiled=True),
    )
    cot_rows = jnp.dot(select, cotangent, preferred_element_type=jnp.float32)
    grad_rate = jnp.sum(cot_rows * update, axis=-1)
    grad_update = cot_rows * router_rate[:, None]
    grad_expanded = grad_update.astype(jnp.bfloat16)
    grad_down = jnp.einsum("kf,kd->fd", active, grad_expanded, preferred_element_type=jnp.float32)
    grad_active = jnp.einsum(
        "kd,fd->kf", grad_expanded, w_down_back, preferred_element_type=jnp.float32
    )
    (grad_inner_float,) = gelu_pull(grad_active)
    grad_inner = grad_inner_float.astype(jnp.bfloat16)
    grad_up = jnp.einsum("kd,kf->df", normed_two, grad_inner, preferred_element_type=jnp.float32)
    grad_normed_two = jnp.einsum(
        "kf,df->kd", grad_inner, w_in_back, preferred_element_type=jnp.float32
    )
    grad_middle, grad_gain_two = middle_pull(grad_normed_two)
    grad_attended = (grad_update + grad_middle).astype(jnp.bfloat16)
    grad_proj = jnp.einsum("ka,kd->ad", attn_mix, grad_attended, preferred_element_type=jnp.float32)
    grad_mix = jnp.einsum(
        "kd,ad->ka", grad_attended, w_out_back, preferred_element_type=jnp.float32
    ).astype(jnp.bfloat16)
    grad_mix_heads = split_heads(grad_mix)
    scores_again = masked_scores(query_heads, key_heads, allowed, score_scale)
    prob_float = jnp.where(allowed[None], jnp.exp(scores_again - log_total), 0.0)
    grad_probs = jnp.einsum(
        "qhd,khd->hqk", grad_mix_heads, value_heads, preferred_element_type=jnp.float32
    )
    row_delta = jnp.sum(prob_float * grad_probs, axis=-1, keepdims=True)
    grad_scores = (prob_float * (grad_probs - row_delta)).astype(jnp.bfloat16)
    prob_low = prob_float.astype(jnp.bfloat16)
    grad_query = (
        jnp.einsum("hqk,khd->qhd", grad_scores, key_heads, preferred_element_type=jnp.float32)
        * score_scale
    )
    grad_key = (
        jnp.einsum("hqk,qhd->khd", grad_scores, query_heads, preferred_element_type=jnp.float32)
        * score_scale
    )
    grad_value = jnp.einsum(
        "hqk,qhd->khd", prob_low, grad_mix_heads, preferred_element_type=jnp.float32
    )
    grad_qkv = jnp.concatenate(
        [
            grad_query.reshape(row_count, model_width),
            grad_key.reshape(row_count, model_width),
            grad_value.reshape(row_count, model_width),
        ],
        axis=1,
    ).astype(jnp.bfloat16)
    grad_proj_in = jnp.einsum("kd,ke->de", normed, grad_qkv, preferred_element_type=jnp.float32)
    grad_normed = jnp.einsum("ke,de->kd", grad_qkv, w_qkv_back, preferred_element_type=jnp.float32)
    grad_routed_norm, grad_gain_one = norm_pull(grad_normed)
    grad_routed = (
        grad_routed_norm + grad_middle + grad_rate[:, None] * router.astype(jnp.float32)
    ).astype(jnp.bfloat16)
    grad_tokens = (
        cotangent.astype(jnp.float32)
        + jnp.einsum("kt,kd->td", select, grad_routed, preferred_element_type=jnp.float32)
    ).astype(jnp.bfloat16)
    router_local = jnp.dot(grad_rate, routed, precision=lax.Precision.HIGHEST)
    shard_up, shard_down, shard_gain_two = (
        lax.psum_scatter(grad_up, "fsdp", scatter_dimension=0, tiled=True),
        lax.psum_scatter(grad_down, "fsdp", scatter_dimension=0, tiled=True),
        lax.psum_scatter(grad_gain_two, "fsdp", scatter_dimension=0, tiled=True),
    )
    shard_qkv, shard_proj, shard_gain_one = (
        lax.psum_scatter(grad_proj_in, "fsdp", scatter_dimension=0, tiled=True),
        lax.psum_scatter(grad_proj, "fsdp", scatter_dimension=0, tiled=True),
        lax.psum_scatter(grad_gain_one, "fsdp", scatter_dimension=0, tiled=True),
    )
    summed = (
        lax.psum(shard_qkv.astype(jnp.bfloat16), "dp").astype(jnp.float32),
        lax.psum(shard_proj.astype(jnp.bfloat16), "dp").astype(jnp.float32),
        lax.psum(shard_up.astype(jnp.bfloat16), "dp").astype(jnp.float32),
        lax.psum(shard_down.astype(jnp.bfloat16), "dp").astype(jnp.float32),
        lax.psum(shard_gain_one.astype(jnp.bfloat16), "dp").astype(jnp.float32),
        lax.psum(shard_gain_two.astype(jnp.bfloat16), "dp").astype(jnp.float32),
    )
    grad_router = lax.psum(router_local, ("fsdp", "dp"))
    return (
        output,
        grad_tokens,
        summed[0],
        summed[1],
        summed[2],
        summed[3],
        summed[4],
        summed[5],
        grad_router,
    )


def solution(mesh):
    placed = (
        P(("fsdp", "dp"), None),
        P(("fsdp", "dp"), None),
        P(("fsdp", "dp")),
        P(("fsdp", "dp")),
        P("fsdp", None),
        P("fsdp", None),
        P("fsdp", None),
        P("fsdp", None),
        P("fsdp"),
        P("fsdp"),
        P(),
    )
    return jax.shard_map(
        per_device,
        mesh=mesh,
        in_specs=placed,
        out_specs=(
            P(("fsdp", "dp"), None),
            P(("fsdp", "dp"), None),
            P("fsdp", None),
            P("fsdp", None),
            P("fsdp", None),
            P("fsdp", None),
            P("fsdp"),
            P("fsdp"),
            P(),
        ),
        check_vma=False,
    )
```

profile of v0, /device:TPU:0, one launch (start us, length us, event | category | flops | bytes accessed | tf_op | source)
XLA Modules:
  0.0 773.5 jit_solution(13917479941379814595)
XLA Ops:
  7.2 0.7 all-gather.7.cloned.1.call-update
  8.0 0.7 all-gather.9.cloned.1.call-update
  8.7 0.7 all-gather.11.cloned.1.call-update
  9.4 0.5 all-gather.13.cloned.1.call-update
  10.0 10.4 %all-gather = bf16[8,1,128]{2,1,0:T(2,128)(2,1)S(1)} all-gather(bf16[1,1,128]{2,1,0:T(2,128)(2,1)} %bitcast.84), channel_id=1, replica_groups=mesh['fsdp'=8,'dp'=4] {'fsdp'}, dimensions={0}, use_global_device_ids=true | all-gather | bytes 2304 | tf_op jit(solution)/shard_map/all_gather | solution.py:53
  20.4 8.9 %all-gather.1 = bf16[8,1,128]{2,1,0:T(2,128)(2,1)S(1)} all-gather(bf16[1,1,128]{2,1,0:T(2,128)(2,1)} %bitcast.85), channel_id=1, replica_groups=mesh['fsdp'=8,'dp'=4] {'fsdp'}, dimensions={0}, use_global_device_ids=true | all-gather | bytes 2304 | tf_op jit(solution)/shard_map/all_gather | solution.py:54
  29.3 0.7 reshape.191
  30.0 0.8 reduce-window.8
  30.8 0.8 convert_reduce_fusion
  31.6 7.8 %multiply_reduce_fusion.7 = (f32[512]{0:T(512)S(1)}, f32[512,1024]{1,0:T(8,128)S(1)}) fusion(bf16[4096,1024]{1,0:T(8,128)(2,1)} %param.11, s32[512]{0:T(512)} %param.14), kind=kOutput, calls=%fused_computation.51 | convolution fusion | flops 4298112512 | bytes 10489856 | tf_op jit(solution)/shard_map/dot_general | solution.py:64
  39.4 0.3 compare_and_fusion
  39.7 0.4 fusion.36
  40.1 9.3 %fusion.12 = f32[512,1024]{1,0:T(8,128)} fusion(bf16[4096,1024]{1,0:T(8,128)(2,1)} %param.12, s32[512]{0:T(512)S(1)} %copy-done.10), kind=kOutput, calls=%fused_computation.24 | convolution fusion | flops 4297064448 | bytes 10487808 | tf_op jit(solution)/shard_map/dot_general | solution.py:106
  49.4 8.7 %all-gather.7.cloned.1.call-done = bf16[1024,3072]{1,0:T(8,128)(2,1)} async-done(((bf16[128,3072]{1,0:T(8,128)(2,1)}), bf16[1024,3072]{1,0:T(8,128)(2,1)}) %all-gather.7.cloned.1.call-update) | async-done | bytes 6291472 | tf_op jit(solution)/shard_map/all_gather | solution.py:51
  58.0 6.6 convolution_convert_fusion
  64.6 1.7 fusion.51
  66.4 1.5 copy.50
  67.9 2.3 copy.49
  70.2 2.3 copy.48
  72.4 9.1 %fusion.1 = (f32[16,512]{1,0:T(8,128)S(1)}, f32[16,512,512]{1,2,0:T(8,128)}) fusion(pred[512,512]{0,1:T(8,128)(4,1)S(1)} %compare_and_fusion, bf16[512,16,64]{0,2,1:T(8,128)(2,1)} %bitcast.57, bf16[512,16,64]{0,2,1:T(8,128)(2,1)S(1)} %bitcast.55), kind=kOutput, calls=%fused_computation.11 | convolution fusion | flops 549445632 | bytes 19169280 | tf_op jit(solution)/shard_map/qhd,khd->hqk/dot_general | solution.py:28
  81.5 9.3 %fusion = f32[16,512]{1,0:T(8,128)S(1)} fusion(f32[16,512,512]{1,2,0:T(8,128)} %get-tuple-element.31, f32[16,512]{1,0:T(8,128)S(1)} %get-tuple-element.30, pred[512,512]{0,1:T(8,128)(4,1)S(1)} %compare_and_fusion), kind=kLoop, calls=%fused_computation.8 | loop fusion | flops 16769024 | bytes 17104896 | tf_op jit(solution)/shard_map/reduce_sum | solution.py:77
  90.8 9.6 %fusion.23 = bf16[16,64,512]{2,1,0:T(8,128)(2,1)} fusion(bf16[512,16,64]{0,2,1:T(8,128)(2,1)} %bitcast.65, f32[16,512,512]{1,2,0:T(8,128)} %get-tuple-element.31, f32[16,512]{1,0:T(8,128)S(1)} %fusion, f32[16,512]{1,0:T(8,128)S(1)} %get-tuple-element.30, pred[512,512]{0,1:T(8,128)(4,1)S(1)} %compare_and_fusion), kind=kOutput, calls=%fused_computation.54 | convolution fusion | flops 558366720 | bytes 19202048 | tf_op jit(solution)/shard_map/hqk,khd->qhd/dot_general | solution.py:80
  100.4 5.2 multiply_reduce_fusion.6
  105.6 38.3 %all-gather.11.cloned.1.call-done = bf16[1024,4096]{1,0:T(8,128)(2,1)} async-done(((bf16[128,4096]{1,0:T(8,128)(2,1)}), bf16[1024,4096]{1,0:T(8,128)(2,1)}) %all-gather.11.cloned.1.call-update) | async-done | bytes 8388624 | tf_op jit(solution)/shard_map/all_gather | solution.py:57
  143.9 12.1 %fusion.50 = f32[512,4096]{1,0:T(8,128)} fusion(bf16[1024,4096]{1,0:T(8,128)(2,1)} %all-gather.11.cloned.1.call-done, f32[512,1024]{1,0:T(8,128)} %get-tuple-element.22, f32[1024]{0:T(1024)S(1)} %bitcast.74, f32[512]{0:T(512)S(1)} %fusion.39), kind=kOutput, calls=%fused_computation.88 | convolution fusion | flops 4296540160 | bytes 18880512 | tf_op jit(solution)/shard_map/dot_general | solution.py:88
  156.0 44.0 %all-gather.13.cloned.1.call-done = bf16[4096,1024]{1,0:T(8,128)(2,1)} async-done(((bf16[512,1024]{1,0:T(8,128)(2,1)}), bf16[4096,1024]{1,0:T(8,128)(2,1)}) %all-gather.13.cloned.1.call-update) | async-done | bytes 8388624 | tf_op jit(solution)/shard_map/all_gather | solution.py:58
  200.0 14.6 %fusion.8 = bf16[512,4096]{1,0:T(8,128)(2,1)} fusion(f32[512,4096]{1,0:T(8,128)} %fusion.50, bf16[4096,1024]{1,0:T(8,128)(2,1)} %all-gather.13.cloned.1.call-done, f32[512,1024]{1,0:T(8,128)} %fusion.12, f32[512]{0:T(512)S(1)} %bitcast.79), kind=kOutput, calls=%fused_computation.18 | convolution fusion | flops 4337958912 | bytes 23070720 | tf_op jit(solution)/shard_map/kd,fd->kf/dot_general | solution.py:111
  214.6 10.9 %multiply_reduce_fusion.1 = (f32[1024]{0:T(1024)S(1)}, f32[512]{0:T(512)S(1)}, f32[512,1024]{1,0:T(8,128)}) fusion(f32[512,1024]{1,0:T(8,128)S(1)} %copy-done.1, f32[512]{0:T(512)S(1)} %fusion.39, f32[1024]{0:T(1024)S(1)} %bitcast.75, bf16[512,4096]{1,0:T(8,128)(2,1)} %fusion.8, bf16[1024,4096]{1,0:T(8,128)(2,1)} %all-gather.11.cloned.1.call-done), kind=kOutput, calls=%fused_computation.39 | convolution fusion | flops 4298111488 | bytes 16789504 | tf_op jit(solution)/shard_map/kf,df->kd/dot_general | solution.py:117
  225.5 10.1 %multiply_reduce_fusion.3 = (f32[512]{0:T(512)S(1)}, bf16[512,1024]{1,0:T(8,128)(2,1)S(1)}, f32[512,1024]{1,0:T(8,128)}) fusion(f32[512,1024]{1,0:T(8,128)S(1)} %copy-done.19, f32[512,1024]{1,0:T(8,128)S(1)} %copy-done.1, f32[512]{0:T(512)S(1)} %multiply_multiply_fusion.3, f32[512]{0:T(512)S(1)} %fusion.39, f32[512,1024]{1,0:T(8,128)} %get-tuple-element.33, ...), kind=kOutput, calls=%fused_computation.41 | convolution fusion | flops 4319608320 | bytes 28323840 | tf_op jit(solution)/shard_map/dot_general | solution.py:91
  235.6 1.0 copy-done.18
  236.6 3.2 fusion.52
  239.8 4.2 convolution_convert_fusion.1
  244.0 2.3 copy.52
  246.4 13.6 %multiply_reduce_fusion = (f32[16,512]{1,0:T(8,128)S(1)}, f32[16,512,512]{1,2,0:T(8,128)}) fusion(f32[16,512]{1,0:T(8,128)S(1)} %log_add_fusion, f32[16,512,512]{1,2,0:T(8,128)} %get-tuple-element.31, pred[512,512]{0,1:T(8,128)(4,1)S(1)} %compare_and_fusion, bf16[512,16,64]{0,2,1:T(8,128)(2,1)} %bitcast.67, bf16[512,16,64]{0,2,1:T(8,128)(2,1)} %bitcast.66), kind=kOutput, calls=%fused_computation.2 | convolution fusion | flops 562028544 | bytes 35979264 | tf_op jit(solution)/shard_map/qhd,khd->hqk/dot_general | solution.py:129
  259.9 13.2 %multiply_convert_fusion = bf16[16,512,512]{1,2,0:T(8,128)(2,1)S(1)} fusion(f32[16,512,512]{1,2,0:T(8,128)} %get-tuple-element.36, f32[16,512]{1,0:T(8,128)S(1)} %get-tuple-element.35, f32[16,512]{1,0:T(8,128)S(1)} %log_add_fusion, f32[16,512,512]{1,2,0:T(8,128)} %get-tuple-element.31, pred[512,512]{0,1:T(8,128)(4,1)S(1)} %compare_and_fusion), kind=kLoop, calls=%fused_computation.1 | loop fusion | flops 29360128 | bytes 42270720 | tf_op jit(solution)/shard_map/convert_element_type | solution.py:133
  273.1 2.6 multiply_convert_fusion.2
  275.8 1.5 multiply_convert_fusion.3
  277.4 8.6 %fusion.24 = bf16[16,64,512]{2,1,0:T(8,128)(2,1)S(1)} fusion(bf16[512,16,64]{0,2,1:T(8,128)(2,1)S(1)} %bitcast.68, f32[16,512]{1,0:T(8,128)S(1)} %log_add_fusion, f32[16,512,512]{1,2,0:T(8,128)} %get-tuple-element.31, pred[512,512]{0,1:T(8,128)(4,1)S(1)} %compare_and_fusion), kind=kOutput, calls=%fused_computation.56 | convolution fusion | flops 558366720 | bytes 19169280 | tf_op jit(solution)/shard_map/hqk,qhd->khd/dot_general | solution.py:143
  286.0 0.9 copy-done.16
  287.0 9.9 %fusion.27 = f32[1024,3072]{1,0:T(8,128)} fusion(bf16[512,1024]{0,1:T(8,128)(2,1)S(1)} %bitcast.88, bf16[512,1024]{0,1:T(8,128)(2,1)S(1)} %bitcast.63, bf16[512,1024]{0,1:T(8,128)(2,1)S(1)} %bitcast.59, f32[512,1024]{1,0:T(8,128)S(1)} %get-tuple-element.29, f32[1024]{0:T(1024)S(1)} %bitcast.71, f32[512]{0:T(512)S(1)} %fusion.38), kind=kOutput, calls=%fused_computation.57 | convolution fusion | flops 3232235520 | bytes 17831936 | tf_op jit(solution)/shard_map/kd,ke->de/dot_general | solution.py:154
  296.9 19.0 %fusion.47 = f32[4096,1024]{1,0:T(8,128)} fusion(f32[512,1024]{1,0:T(8,128)} %fusion.12, f32[512]{0:T(512)S(1)} %bitcast.81, f32[512,4096]{1,0:T(8,128)} %fusion.50), kind=kOutput, calls=%fused_computation.85 | convolution fusion | flops 4314890240 | bytes 27265024 | tf_op jit(solution)/shard_map/kf,kd->fd/dot_general | solution.py:110
  316.2 15.3 %fusion.49 = f32[1024,4096]{1,0:T(8,128)} fusion(bf16[512,4096]{1,0:T(8,128)(2,1)} %fusion.8, f32[512,1024]{1,0:T(8,128)} %get-tuple-element.22, f32[1024]{0:T(1024)S(1)} %bitcast.77, f32[512]{0:T(512)S(1)} %fusion.39), kind=kOutput, calls=%fused_computation.87 | convolution fusion | flops 4296540160 | bytes 23074816 | tf_op jit(solution)/shard_map/kd,kf->df/dot_general | solution.py:116
  331.6 0.6 copy-done.12
  332.2 0.6 dynamic-slice
  333.5 8.4 %multiply_reduce_fusion.2 = (f32[1024]{0:T(1024)S(1)}, f32[512]{0:T(512)S(1)}, f32[512,1024]{1,0:T(8,128)}) fusion(f32[512,1024]{1,0:T(8,128)S(1)} %get-tuple-element.29, f32[512]{0:T(512)S(1)} %fusion.38, f32[1024]{0:T(1024)S(1)} %bitcast.72, bf16[1024,3072]{1,0:T(8,128)(2,1)} %all-gather.7.cloned.1.call-done, bf16[512,1024]{0,1:T(8,128)(2,1)} %bitcast.89, ...), kind=kOutput, calls=%fused_computation.40 | convolution fusion | flops 3233806848 | bytes 13643776 | tf_op jit(solution)/shard_map/ke,de->kd/dot_general | solution.py:155
  341.9 15.5 %all-reduce.2 = (bf16[1024]{0:T(1024)(128)(2,1)S(1)}, bf16[1024]{0:T(1024)(128)(2,1)S(1)}) all-reduce(f32[1024]{0:T(1024)S(1)} %get-tuple-element.11, f32[1024]{0:T(1024)S(1)} %get-tuple-element.9), channel_id=6, replica_groups=mesh['fsdp'=8,'dp'=4] {'fsdp'}, use_global_device_ids=true, to_apply=%region_19.20.clone | all-reduce | flops 2048 | bytes 12288
  357.6 11.7 %all-reduce.3 = (bf16[128]{0:T(256)(128)(2,1)S(1)}, bf16[128]{0:T(256)(128)(2,1)S(1)}) all-reduce(bf16[128]{0:T(256)(128)(2,1)S(1)} %dynamic-slice.7, bf16[128]{0:T(256)(128)(2,1)S(1)} %dynamic-slice.6), channel_id=1, replica_groups=mesh['fsdp'=8,'dp'=4] {'dp'}, use_global_device_ids=true, to_apply=%region_20.21 | all-reduce | flops 256 | bytes 1024 | tf_op jit(solution)/shard_map/psum | solution.py:180
  369.3 0.5 convert_element_type.147
  369.8 0.5 convert_element_type.149
  370.3 1.1 fusion.53
  371.4 37.7 %psum.55 = f32[1024]{0:T(1024)} all-reduce(f32[1024]{0:T(1024)S(1)} %bitcast.69), channel_id=1, replica_groups=mesh['fsdp'=8,'dp'=4] {'fsdp','dp'}, use_global_device_ids=true, to_apply=%region_24.25 | all-reduce | flops 1024 | bytes 8192 | tf_op jit(solution)/shard_map/psum | solution.py:183
  409.2 1.8 convert_element_type.140
  411.1 2.6 convert_element_type.138
  413.7 100.4 %reduce-scatter.11.cloned.1.call-done = f32[512,1024]{1,0:T(8,128)} async-done(((f32[4096,1024]{1,0:T(8,128)}), f32[512,1024]{1,0:T(8,128)}) %reduce-scatter.11.cloned.1.call-update) | async-done | bytes 2097168 | tf_op jit(solution)/shard_map/reduce_scatter | solution.py:167
  514.0 2.7 convert_element_type.144
  516.8 117.0 %reduce-scatter.9.cloned.1.call-done = f32[128,4096]{1,0:T(8,128)} async-done(((f32[1024,4096]{1,0:T(8,128)}), f32[128,4096]{1,0:T(8,128)}) %reduce-scatter.9.cloned.1.call-update) | async-done | bytes 2097168 | tf_op jit(solution)/shard_map/reduce_scatter | solution.py:166
  633.8 2.7 convert_element_type.142
  636.6 10.0 %add_convert_fusion.1 = bf16[4096,1024]{1,0:T(8,128)(2,1)} fusion(bf16[4096,1024]{1,0:T(8,128)(2,1)} %param.11, s32[512]{0:T(512)S(1)} %copy-done.11, f32[512,1024]{1,0:T(8,128)} %get-tuple-element.34, f32[512]{0:T(512)S(1)} %bitcast.82), kind=kOutput, calls=%fused_computation.4 | convolution fusion | flops 4310695936 | bytes 18878464 | tf_op jit(solution)/shard_map/kt,kd->td/dot_general | solution.py:96
  646.6 11.4 %add_convert_fusion = bf16[4096,1024]{1,0:T(8,128)(2,1)} fusion(bf16[4096,1024]{1,0:T(8,128)(2,1)} %param.12, s32[512]{0:T(512)S(1)} %copy-done.11, f32[512,1024]{1,0:T(8,128)S(1)} %get-tuple-element.29, f32[512,1024]{1,0:T(8,128)S(1)} %copy-done.20, f32[1024]{0:T(1024)S(1)} %convert_element_type.135, f32[512]{0:T(512)S(1)} %get-tuple-element.26, ...), kind=kOutput, calls=%fused_computation | convolution fusion | flops 4316987392 | bytes 25190400 | tf_op jit(solution)/shard_map/kt,kd->td/dot_general | solution.py:162
  658.0 100.1 %all-reduce.7.cloned.1.call-done = (bf16[128,3072]{1,0:T(8,128)(2,1)}, bf16[128,1024]{1,0:T(8,128)(2,1)}, bf16[128,4096]{1,0:T(8,128)(2,1)}, bf16[512,1024]{1,0:T(8,128)(2,1)}) async-done(((bf16[128,3072]{1,0:T(8,128)(2,1)}, bf16[128,1024]{1,0:T(8,128)(2,1)}, bf16[128,4096]{1,0:T(8,128)(2,1)}, bf16[512,1024]{1,0:T(8,128)(2,1)}), (bf16[128,3072]{1,0:T(8,128)(2,1)}, bf16[128,1024]{1,0:T(8,128)(2,1)}, ...) | async-done | bytes 3145744 | tf_op jit(solution)/shard_map/psum | solution.py:176
  758.1 1.9 convert_element_type.141
  760.0 2.4 convert_element_type.139
  762.5 2.8 convert_element_type.143
  765.2 1.6 convert_element_type.145
  (68 shorter events, 1.1 us)
Async XLA Ops:
  7.2 50.9 %all-gather.7.cloned.1.call-start = ((), (), s32[]{:S(2)}) async-start(), calls=%async_computation.4 | async-start | bytes 7077888 | tf_op jit(solution)/shard_map/all_gather | solution.py:51
  7.9 92.5 %all-gather.9.cloned.1.call-start = ((), (), s32[]{:S(2)}) async-start(), calls=%async_computation.5 | async-start | bytes 2359296 | tf_op jit(solution)/shard_map/all_gather | solution.py:52
  8.7 135.3 %all-gather.11.cloned.1.call-start = ((), (), s32[]{:S(2)}) async-start(), calls=%async_computation.6 | async-start | bytes 9437184 | tf_op jit(solution)/shard_map/all_gather | solution.py:57
  9.4 190.6 %all-gather.13.cloned.1.call-start = ((), (), s32[]{:S(2)}) async-start(), calls=%async_computation.7 | async-start | bytes 9437184 | tf_op jit(solution)/shard_map/all_gather | solution.py:58
  10.0 399.2 %reduce-scatter.7.cloned.1.call-start = ((), (), s32[]{:S(2)}) async-start(), calls=%async_computation.9 | async-start | bytes 4718592 | tf_op jit(solution)/shard_map/reduce_scatter | solution.py:172
  31.6 7.8 %copy-start.10 = (s32[512]{0:T(512)S(1)}, s32[512]{0:T(512)}, u32[]{:S(2)}) copy-start(s32[512]{0:T(512)} %param.14) | copy-start | bytes 6148
  39.4 0.7 copy-start.13
  200.0 14.6 %copy-start.1 = (f32[512,1024]{1,0:T(8,128)S(1)}, f32[512,1024]{1,0:T(8,128)}, u32[]{:S(2)}) copy-start(f32[512,1024]{1,0:T(8,128)} %get-tuple-element.22) | copy-start | bytes 6291460
  214.6 10.9 %copy-start.3 = (f32[512,1024]{1,0:T(8,128)S(1)}, f32[512,1024]{1,0:T(8,128)}, u32[]{:S(2)}) copy-start(f32[512,1024]{1,0:T(8,128)} %get-tuple-element.32) | copy-start | bytes 6291460
  214.6 10.9 %copy-start.15 = (bf16[4096,1024]{1,0:T(8,128)(2,1)S(1)}, bf16[4096,1024]{1,0:T(8,128)(2,1)}, u32[]{:S(2)}) copy-start(bf16[4096,1024]{1,0:T(8,128)(2,1)} %all-gather.13.cloned.1.call-done) | copy-start | bytes 25165828
  214.6 10.9 %copy-start.19 = (f32[512,1024]{1,0:T(8,128)S(1)}, f32[512,1024]{1,0:T(8,128)}, u32[]{:S(2)}) copy-start(f32[512,1024]{1,0:T(8,128)} %fusion.12) | copy-start | bytes 6291460
  225.5 11.1 %copy-start.6 = (bf16[16,64,512]{2,1,0:T(8,128)(2,1)S(1)}, bf16[16,64,512]{2,1,0:T(8,128)(2,1)}, u32[]{:S(2)}) copy-start(bf16[16,64,512]{2,1,0:T(8,128)(2,1)} %fusion.23) | copy-start | bytes 3145732
  235.6 1.0 copy-start.18
  246.3 164.7 %reduce-scatter.5.cloned.1.call-start = ((), (), s32[]{:S(2)}) async-start(), calls=%async_computation.8 | async-start | bytes 14155776 | tf_op jit(solution)/shard_map/reduce_scatter | solution.py:171
  259.9 13.2 %copy-start = (bf16[512,1024]{0,1:T(8,128)(2,1)S(1)}, bf16[512,1024]{0,1:T(8,128)(2,1)}, u32[]{:S(2)}) copy-start(bf16[512,1024]{0,1:T(8,128)(2,1)} %copy.49) | copy-start | bytes 3145732
  275.7 10.3 %copy-start.7 = (bf16[16,64,512]{2,1,0:T(8,128)(2,1)}, bf16[16,64,512]{2,1,0:T(8,128)(2,1)S(1)}, u32[]{:S(2)}) copy-start(bf16[16,64,512]{2,1,0:T(8,128)(2,1)S(1)} %multiply_convert_fusion.2) | copy-start | bytes 3145732
  275.8 1.6 copy-start.9
  277.4 8.7 %copy-start.4 = (bf16[16,64,512]{2,1,0:T(8,128)(2,1)}, bf16[16,64,512]{2,1,0:T(8,128)(2,1)S(1)}, u32[]{:S(2)}) copy-start(bf16[16,64,512]{2,1,0:T(8,128)(2,1)S(1)} %multiply_convert_fusion.3) | copy-start | bytes 3145732
  286.0 1.0 copy-start.16
  296.9 217.2 %reduce-scatter.11.cloned.1.call-start = ((), (), s32[]{:S(2)}) async-start(), calls=%async_computation.11 | async-start | bytes 18874368 | tf_op jit(solution)/shard_map/reduce_scatter | solution.py:167
  316.0 317.8 %reduce-scatter.9.cloned.1.call-start = ((), (), s32[]{:S(2)}) async-start(), calls=%async_computation.10 | async-start | bytes 18874368 | tf_op jit(solution)/shard_map/reduce_scatter | solution.py:166
  331.5 0.7 copy-start.12
  331.5 0.7 copy-start.17
  331.5 1.9 copy-start.5
  331.6 426.6 %all-reduce.7.cloned.1.call-start = ((), (), s32[]{:S(2)}) async-start(), calls=%async_computation.12 | async-start | bytes 6291456 | tf_op jit(solution)/shard_map/psum | solution.py:176
  333.5 75.7 %copy-start.14 = (f32[512]{0:T(512)S(1)}, f32[512]{0:T(512)}, u32[]{:S(2)}) copy-start(f32[512]{0:T(512)} %copy-done.13) | copy-start | bytes 6148
  409.2 227.4 %copy-start.11 = (s32[512]{0:T(512)S(1)}, s32[512]{0:T(512)}, u32[]{:S(2)}) copy-start(s32[512]{0:T(512)} %param.14) | copy-start | bytes 6148
  636.5 10.1 %copy-start.2 = (f32[512,1024]{1,0:T(8,128)S(1)}, f32[512,1024]{1,0:T(8,128)}, u32[]{:S(2)}) copy-start(f32[512,1024]{1,0:T(8,128)} %get-tuple-element.22) | copy-start | bytes 6291460
  636.6 10.1 %copy-start.20 = (f32[512,1024]{1,0:T(8,128)S(1)}, f32[512,1024]{1,0:T(8,128)}, u32[]{:S(2)}) copy-start(f32[512,1024]{1,0:T(8,128)} %get-tuple-element.37) | copy-start | bytes 6291460
  636.6 10.0 %copy-start.21 = (f32[512,1024]{1,0:T(8,128)S(1)}, f32[512,1024]{1,0:T(8,128)}, u32[]{:S(2)}) copy-start(f32[512,1024]{1,0:T(8,128)} %get-tuple-element.33) | copy-start | bytes 6291460
  758.1 7.1 copy-start.8
Sparse Core Ops, SparseCore 0:
  9.9 48.1 all-gather.6
  59.9 27.7 all-gather.8
  89.6 54.2 all-gather.10
  145.7 54.2 all-gather.12
  246.4 51.1 reduce-scatter.6
  301.0 93.5 reduce-scatter.4
  398.2 115.8 reduce-scatter.10
  517.6 116.1 reduce-scatter.8
  637.0 121.0 all-reduce.6
where the time goes:
time: 783 us; the launch traced here: 774 us
  waiting for transfers between devices  411 us (52%)
  matrix products  204 us (26%)
  blocking collectives  84.2 us (11%)
  other arithmetic  44 us (6%)
  between operations  15 us (2%)
  local copies, waits for them, and re-layouts  14.3 us (2%)
    reduce_scatter x1, waiting for transfers between devices, per_device(): lax.psum_scatter(grad_up, 'fsdp', scatter_dimension=0, tiled=True)  117 us
    reduce_scatter x1, waiting for transfers between devices, per_device(): lax.psum_scatter(grad_down, 'fsdp', scatter_dimension=0, tiled=True)  100 us
    psum x1, waiting for transfers between devices, per_device(): lax.psum(shard_qkv.astype(jnp.bfloat16), 'dp').astype(jnp.float32)  100 us
    all_gather x1, waiting for transfers between devices, per_device(): lax.all_gather(mlp_out, 'fsdp', axis=0, tiled=True)  44 us
    all_gather x1, waiting for transfers between devices, per_device(): lax.all_gather(mlp_in, 'fsdp', axis=0, tiled=True)  38.3 us
    psum x1, blocking collectives, per_device(): grad_router = lax.psum(router_local, ('fsdp', 'dp'))  37.7 us
    dot_general x1, matrix products, per_device(): jnp.einsum('kf,kd->fd', active, grad_expanded, preferred_element_type=jnp...  19 us
  transfers between devices with their start and end apart: 9, of which 6 were waited for; matrix products, arithmetic and copies ran while one was open for 26% of the time, Pallas kernels for 0%

commit v1 on v0

--- a/solution.py
+++ b/solution.py
@@ -2,11 +2,13 @@
 import jax.numpy as jnp
 from jax import lax
 from jax.sharding import PartitionSpec as P
+from jax.lax import all_gather
 
 HEADS = 16
 HEAD = 64
 EPS = 1e-06
 MASKED = -1e30
+marks_order = lambda field: jnp.sum(all_gather(field, "dp"), axis=0)
 
 
 def rms_scale(values, gain_vec):
@@ -173,7 +175,7 @@
         lax.psum_scatter(grad_gain_one, "fsdp", scatter_dimension=0, tiled=True),
     )
     summed = (
-        lax.psum(shard_qkv.astype(jnp.bfloat16), "dp").astype(jnp.float32),
+        marks_order(shard_qkv.astype(jnp.bfloat16)).astype(jnp.float32),
         lax.psum(shard_proj.astype(jnp.bfloat16), "dp").astype(jnp.float32),
         lax.psum(shard_up.astype(jnp.bfloat16), "dp").astype(jnp.float32),
         lax.psum(shard_down.astype(jnp.bfloat16), "dp").astype(jnp.float32),

time: 783 us -> 864 us (1.10)
  waiting for transfers between devices: 411 us -> 489 us
    reduce_scatter x1, waiting for transfers between devices: 0.01 us -> 55.1 us  [per_device(): lax.psum_scatter(grad_proj_in, 'fsdp', scatter_dimension=0, tiled=True)]
    reduce_scatter x1, waiting for transfers between devices: 100 us -> 118 us  [per_device(): lax.psum_scatter(grad_down, 'fsdp', scatter_dimension=0, tiled=True)]
  transfers between devices with their start and end apart: 9 -> 10, of which waited for: 6 -> 9; matrix products, arithmetic and copies ran while one was open for 26% -> 19% of each run, Pallas kernels for 0% -> 0%
where the time goes in v1:
time: 864 us; the launch traced here: 855 us
  waiting for transfers between devices  489 us (57%)
  matrix products  203 us (23%)
  blocking collectives  86.7 us (10%)
  other arithmetic  45.5 us (5%)
  between operations  15.4 us (2%)
  local copies, waits for them, and re-layouts  14.7 us (2%)
    reduce_scatter x1, waiting for transfers between devices, per_device(): lax.psum_scatter(grad_down, 'fsdp', scatter_dimension=0, tiled=True)  118 us
    reduce_scatter x1, waiting for transfers between devices, per_device(): lax.psum_scatter(grad_up, 'fsdp', scatter_dimension=0, tiled=True)  117 us
    psum x1, waiting for transfers between devices, per_device(): lax.psum(shard_proj.astype(jnp.bfloat16), 'dp').astype(jnp.float32)  92.6 us
    reduce_scatter x1, waiting for transfers between devices, per_device(): lax.psum_scatter(grad_proj_in, 'fsdp', scatter_dimension=0, tiled=True)  55.1 us
    all_gather x1, waiting for transfers between devices, per_device(): lax.all_gather(mlp_out, 'fsdp', axis=0, tiled=True)  44 us
    psum x1, blocking collectives, per_device(): grad_router = lax.psum(router_local, ('fsdp', 'dp'))  42.8 us
    all_gather x1, waiting for transfers between devices, per_device(): lax.all_gather(mlp_in, 'fsdp', axis=0, tiled=True)  38.3 us
    dot_general x1, matrix products, per_device(): jnp.einsum('kf,kd->fd', active, grad_expanded, preferred_element_type=jnp...  17.8 us
  transfers between devices with their start and end apart: 10, of which 9 were waited for; matrix products, arithmetic and copies ran while one was open for 19% of the time, Pallas kernels for 0%

profile of v1, /device:TPU:0, one launch (start us, length us, event | category | flops | bytes accessed | tf_op | source)
XLA Modules:
  0.0 855.1 jit_solution(15725409342789099442)
XLA Ops:
  7.2 0.7 all-gather.9.cloned.1.call-update
  8.0 0.7 all-gather.11.cloned.1.call-update
  8.7 0.7 all-gather.13.cloned.1.call-update
  9.4 0.5 all-gather.15.cloned.1.call-update
  10.0 10.4 %all-gather.1 = bf16[8,1,128]{2,1,0:T(2,128)(2,1)S(1)} all-gather(bf16[1,1,128]{2,1,0:T(2,128)(2,1)} %bitcast.86), channel_id=1, replica_groups=mesh['fsdp'=8,'dp'=4] {'fsdp'}, dimensions={0}, use_global_device_ids=true | all-gather | bytes 2304 | tf_op jit(solution)/shard_map/all_gather | solution.py:55
  20.4 8.9 %all-gather.2 = bf16[8,1,128]{2,1,0:T(2,128)(2,1)S(1)} all-gather(bf16[1,1,128]{2,1,0:T(2,128)(2,1)} %bitcast.87), channel_id=1, replica_groups=mesh['fsdp'=8,'dp'=4] {'fsdp'}, dimensions={0}, use_global_device_ids=true | all-gather | bytes 2304 | tf_op jit(solution)/shard_map/all_gather | solution.py:56
  29.3 0.7 reshape.192
  30.0 0.8 reduce-window.8
  30.8 0.8 convert_reduce_fusion
  31.6 7.8 multiply_reduce_fusion.7
  40.1 9.3 %fusion.12 = f32[512,1024]{1,0:T(8,128)} fusion(bf16[4096,1024]{1,0:T(8,128)(2,1)} %param.12, s32[512]{0:T(512)S(1)} %copy-done.10), kind=kOutput, calls=%fused_computation.24 | convolution fusion | flops 4297064448 | bytes 10487808 | tf_op jit(solution)/shard_map/dot_general | solution.py:108
  49.4 8.7 %all-gather.9.cloned.1.call-done = bf16[1024,3072]{1,0:T(8,128)(2,1)} async-done(((bf16[128,3072]{1,0:T(8,128)(2,1)}), bf16[1024,3072]{1,0:T(8,128)(2,1)}) %all-gather.9.cloned.1.call-update) | async-done | bytes 6291472 | tf_op jit(solution)/shard_map/all_gather | solution.py:53
  58.0 6.6 convolution_convert_fusion
  64.6 1.7 fusion.51
  66.4 1.5 copy.50
  67.9 2.3 copy.49
  70.2 2.3 copy.48
  72.5 9.1 %fusion.1 = (f32[16,512]{1,0:T(8,128)S(1)}, f32[16,512,512]{1,2,0:T(8,128)}) fusion(pred[512,512]{0,1:T(8,128)(4,1)S(1)} %compare_and_fusion, bf16[512,16,64]{0,2,1:T(8,128)(2,1)} %bitcast.58, bf16[512,16,64]{0,2,1:T(8,128)(2,1)S(1)} %bitcast.56), kind=kOutput, calls=%fused_computation.11 | convolution fusion | flops 549445632 | bytes 19169280 | tf_op jit(solution)/shard_map/qhd,khd->hqk/dot_general | solution.py:30
  81.6 9.3 %fusion = f32[16,512]{1,0:T(8,128)S(1)} fusion(f32[16,512,512]{1,2,0:T(8,128)} %get-tuple-element.30, f32[16,512]{1,0:T(8,128)S(1)} %get-tuple-element.29, pred[512,512]{0,1:T(8,128)(4,1)S(1)} %compare_and_fusion), kind=kLoop, calls=%fused_computation.8 | loop fusion | flops 16769024 | bytes 17104896 | tf_op jit(solution)/shard_map/reduce_sum | solution.py:79
  90.9 9.5 %fusion.23 = bf16[16,64,512]{2,1,0:T(8,128)(2,1)} fusion(bf16[512,16,64]{0,2,1:T(8,128)(2,1)} %bitcast.67, f32[16,512,512]{1,2,0:T(8,128)} %get-tuple-element.30, f32[16,512]{1,0:T(8,128)S(1)} %fusion, f32[16,512]{1,0:T(8,128)S(1)} %get-tuple-element.29, pred[512,512]{0,1:T(8,128)(4,1)S(1)} %compare_and_fusion), kind=kOutput, calls=%fused_computation.54 | convolution fusion | flops 558366720 | bytes 19202048 | tf_op jit(solution)/shard_map/hqk,khd->qhd/dot_general | solution.py:82
  100.4 5.2 multiply_reduce_fusion.6
  105.6 38.3 %all-gather.13.cloned.1.call-done = bf16[1024,4096]{1,0:T(8,128)(2,1)} async-done(((bf16[128,4096]{1,0:T(8,128)(2,1)}), bf16[1024,4096]{1,0:T(8,128)(2,1)}) %all-gather.13.cloned.1.call-update) | async-done | bytes 8388624 | tf_op jit(solution)/shard_map/all_gather | solution.py:59
  143.9 12.1 %fusion.50 = f32[512,4096]{1,0:T(8,128)} fusion(bf16[1024,4096]{1,0:T(8,128)(2,1)} %all-gather.13.cloned.1.call-done, f32[512,1024]{1,0:T(8,128)} %get-tuple-element.21, f32[1024]{0:T(1024)S(1)} %bitcast.76, f32[512]{0:T(512)S(1)} %fusion.39), kind=kOutput, calls=%fused_computation.88 | convolution fusion | flops 4296540160 | bytes 18880512 | tf_op jit(solution)/shard_map/dot_general | solution.py:90
  156.0 44.0 %all-gather.15.cloned.1.call-done = bf16[4096,1024]{1,0:T(8,128)(2,1)} async-done(((bf16[512,1024]{1,0:T(8,128)(2,1)}), bf16[4096,1024]{1,0:T(8,128)(2,1)}) %all-gather.15.cloned.1.call-update) | async-done | bytes 8388624 | tf_op jit(solution)/shard_map/all_gather | solution.py:60
  200.0 14.6 %fusion.8 = bf16[512,4096]{1,0:T(8,128)(2,1)} fusion(f32[512,4096]{1,0:T(8,128)} %fusion.50, bf16[4096,1024]{1,0:T(8,128)(2,1)} %all-gather.15.cloned.1.call-done, f32[512,1024]{1,0:T(8,128)} %fusion.12, f32[512]{0:T(512)S(1)} %bitcast.81), kind=kOutput, calls=%fused_computation.18 | convolution fusion | flops 4337958912 | bytes 23070720 | tf_op jit(solution)/shard_map/kd,fd->kf/dot_general | solution.py:113
  214.6 10.9 %multiply_reduce_fusion.1 = (f32[1024]{0:T(1024)S(1)}, f32[512]{0:T(512)S(1)}, f32[512,1024]{1,0:T(8,128)}) fusion(f32[512,1024]{1,0:T(8,128)S(1)} %copy-done.1, f32[512]{0:T(512)S(1)} %fusion.39, f32[1024]{0:T(1024)S(1)} %bitcast.77, bf16[512,4096]{1,0:T(8,128)(2,1)} %fusion.8, bf16[1024,4096]{1,0:T(8,128)(2,1)} %all-gather.13.cloned.1.call-done), kind=kOutput, calls=%fused_computation.39 | convolution fusion | flops 4298111488 | bytes 16789504 | tf_op jit(solution)/shard_map/kf,df->kd/dot_general | solution.py:119
  225.5 10.2 %multiply_reduce_fusion.3 = (f32[512]{0:T(512)S(1)}, bf16[512,1024]{1,0:T(8,128)(2,1)S(1)}, f32[512,1024]{1,0:T(8,128)}) fusion(f32[512,1024]{1,0:T(8,128)S(1)} %copy-done.19, f32[512,1024]{1,0:T(8,128)S(1)} %copy-done.1, f32[512]{0:T(512)S(1)} %multiply_multiply_fusion.3, f32[512]{0:T(512)S(1)} %fusion.39, f32[512,1024]{1,0:T(8,128)} %get-tuple-element.32, ...), kind=kOutput, calls=%fused_computation.41 | convolution fusion | flops 4319608320 | bytes 28323840 | tf_op jit(solution)/shard_map/dot_general | solution.py:93
  235.7 1.0 copy-done.18
  236.6 2.3 convolution_convert_fusion.1
  238.9 2.3 copy.52
  241.2 10.6 %fusion.24 = bf16[16,64,512]{2,1,0:T(8,128)(2,1)S(1)} fusion(bf16[512,16,64]{0,2,1:T(8,128)(2,1)} %bitcast.69, f32[16,512]{1,0:T(8,128)S(1)} %log_add_fusion, f32[16,512,512]{1,2,0:T(8,128)} %get-tuple-element.30, pred[512,512]{0,1:T(8,128)(4,1)S(1)} %compare_and_fusion), kind=kOutput, calls=%fused_computation.56 | convolution fusion | flops 558366720 | bytes 19169280 | tf_op jit(solution)/shard_map/hqk,qhd->khd/dot_general | solution.py:145
  251.8 12.8 %multiply_reduce_fusion = (f32[16,512]{1,0:T(8,128)S(1)}, f32[16,512,512]{1,2,0:T(8,128)}) fusion(f32[16,512]{1,0:T(8,128)S(1)} %log_add_fusion, f32[16,512,512]{1,2,0:T(8,128)} %get-tuple-element.30, pred[512,512]{0,1:T(8,128)(4,1)S(1)} %compare_and_fusion, bf16[512,16,64]{0,2,1:T(8,128)(2,1)S(1)} %bitcast.70, bf16[512,16,64]{0,2,1:T(8,128)(2,1)S(1)} %bitcast.68), kind=kOutput, calls=%fused_computation.2 | convolution fusion | flops 562028544 | bytes 35979264 | tf_op jit(solution)/shard_map/qhd,khd->hqk/dot_general | solution.py:131
  264.6 12.4 %multiply_convert_fusion = bf16[16,512,512]{1,2,0:T(8,128)(2,1)S(1)} fusion(f32[16,512,512]{1,2,0:T(8,128)} %get-tuple-element.35, f32[16,512]{1,0:T(8,128)S(1)} %get-tuple-element.34, f32[16,512]{1,0:T(8,128)S(1)} %log_add_fusion, f32[16,512,512]{1,2,0:T(8,128)} %get-tuple-element.30, pred[512,512]{0,1:T(8,128)(4,1)S(1)} %compare_and_fusion), kind=kLoop, calls=%fused_computation.1 | loop fusion | flops 29360128 | bytes 42270720 | tf_op jit(solution)/shard_map/convert_element_type | solution.py:135
  277.0 2.6 multiply_convert_fusion.2
  279.7 1.5 multiply_convert_fusion.3
  281.2 1.0 copy-done.3
  282.2 9.8 %fusion.27 = f32[1024,3072]{1,0:T(8,128)} fusion(bf16[512,1024]{0,1:T(8,128)(2,1)S(1)} %bitcast.90, bf16[512,1024]{0,1:T(8,128)(2,1)S(1)} %bitcast.65, bf16[512,1024]{0,1:T(8,128)(2,1)S(1)} %bitcast.60, f32[512,1024]{1,0:T(8,128)S(1)} %get-tuple-element.28, f32[1024]{0:T(1024)S(1)} %bitcast.73, f32[512]{0:T(512)S(1)} %fusion.38), kind=kOutput, calls=%fused_computation.57 | convolution fusion | flops 3232235520 | bytes 17831936 | tf_op jit(solution)/shard_map/kd,ke->de/dot_general | solution.py:156
  292.1 1.1 copy-done.5
  293.2 4.5 fusion.52
  297.7 17.8 %fusion.47 = f32[4096,1024]{1,0:T(8,128)} fusion(f32[512,1024]{1,0:T(8,128)} %fusion.12, f32[512]{0:T(512)S(1)} %bitcast.83, f32[512,4096]{1,0:T(8,128)} %fusion.50), kind=kOutput, calls=%fused_computation.85 | convolution fusion | flops 4314890240 | bytes 27265024 | tf_op jit(solution)/shard_map/kf,kd->fd/dot_general | solution.py:112
  315.8 13.4 %fusion.49 = f32[1024,4096]{1,0:T(8,128)} fusion(bf16[512,4096]{1,0:T(8,128)(2,1)} %fusion.8, f32[512,1024]{1,0:T(8,128)} %get-tuple-element.21, f32[1024]{0:T(1024)S(1)} %bitcast.79, f32[512]{0:T(512)S(1)} %fusion.39), kind=kOutput, calls=%fused_computation.87 | convolution fusion | flops 4296540160 | bytes 23074816 | tf_op jit(solution)/shard_map/kd,kf->df/dot_general | solution.py:118
  329.3 55.1 %reduce-scatter.5.cloned.1.call-done = f32[128,3072]{1,0:T(8,128)} async-done(((f32[1024,3072]{1,0:T(8,128)}), f32[128,3072]{1,0:T(8,128)}) %reduce-scatter.5.cloned.1.call-update) | async-done | bytes 1572880 | tf_op jit(solution)/shard_map/reduce_scatter | solution.py:173
  384.4 2.4 convert_element_type.140
  386.9 0.6 dynamic-slice
  388.2 8.4 multiply_reduce_fusion.2
  396.6 12.7 %all-reduce.2 = (bf16[1024]{0:T(1024)(128)(2,1)S(1)}, bf16[1024]{0:T(1024)(128)(2,1)S(1)}) all-reduce(f32[1024]{0:T(1024)S(1)} %get-tuple-element.11, f32[1024]{0:T(1024)S(1)} %get-tuple-element.9), channel_id=7, replica_groups=mesh['fsdp'=8,'dp'=4] {'fsdp'}, use_global_device_ids=true, to_apply=%region_19.20.clone | all-reduce | flops 2048 | bytes 12288
  409.5 11.9 %all-reduce.3 = (bf16[128]{0:T(256)(128)(2,1)S(1)}, bf16[128]{0:T(256)(128)(2,1)S(1)}) all-reduce(bf16[128]{0:T(256)(128)(2,1)S(1)} %dynamic-slice.7, bf16[128]{0:T(256)(128)(2,1)S(1)} %dynamic-slice.6), channel_id=1, replica_groups=mesh['fsdp'=8,'dp'=4] {'dp'}, use_global_device_ids=true, to_apply=%region_20.21 | all-reduce | flops 256 | bytes 1024 | tf_op jit(solution)/shard_map/psum | solution.py:182
  422.4 10.0 %add_convert_fusion.1 = bf16[4096,1024]{1,0:T(8,128)(2,1)} fusion(bf16[4096,1024]{1,0:T(8,128)(2,1)} %param.11, s32[512]{0:T(512)S(1)} %copy-done.11, f32[512,1024]{1,0:T(8,128)} %get-tuple-element.33, f32[512]{0:T(512)S(1)} %bitcast.84), kind=kOutput, calls=%fused_computation.4 | convolution fusion | flops 4310695936 | bytes 18878464 | tf_op jit(solution)/shard_map/kt,kd->td/dot_general | solution.py:98
  432.4 6.4 reduce-scatter.7.cloned.1.call-done
  438.8 1.8 convert_element_type.142
  440.6 118.0 %reduce-scatter.11.cloned.1.call-done = f32[512,1024]{1,0:T(8,128)} async-done(((f32[4096,1024]{1,0:T(8,128)}), f32[512,1024]{1,0:T(8,128)}) %reduce-scatter.11.cloned.1.call-update) | async-done | bytes 2097168 | tf_op jit(solution)/shard_map/reduce_scatter | solution.py:169
  558.6 2.7 convert_element_type.146
  561.3 117.0 %reduce-scatter.9.cloned.1.call-done = f32[128,4096]{1,0:T(8,128)} async-done(((f32[1024,4096]{1,0:T(8,128)}), f32[128,4096]{1,0:T(8,128)}) %reduce-scatter.9.cloned.1.call-update) | async-done | bytes 2097168 | tf_op jit(solution)/shard_map/reduce_scatter | solution.py:168
  678.4 2.8 convert_element_type.144
  681.1 1.1 fusion.53
  682.2 42.8 %psum.47 = f32[1024]{0:T(1024)} all-reduce(f32[1024]{0:T(1024)S(1)} %bitcast.71), channel_id=1, replica_groups=mesh['fsdp'=8,'dp'=4] {'fsdp','dp'}, use_global_device_ids=true, to_apply=%region_24.25 | all-reduce | flops 1024 | bytes 8192 | tf_op jit(solution)/shard_map/psum | solution.py:185
  725.1 12.6 %add_convert_fusion = bf16[4096,1024]{1,0:T(8,128)(2,1)} fusion(bf16[4096,1024]{1,0:T(8,128)(2,1)} %param.12, s32[512]{0:T(512)S(1)} %copy-done.11, f32[512,1024]{1,0:T(8,128)S(1)} %get-tuple-element.28, f32[512,1024]{1,0:T(8,128)} %get-tuple-element.36, f32[1024]{0:T(1024)S(1)} %convert_element_type.137, f32[512]{0:T(512)S(1)} %get-tuple-element.25, ...), kind=kOutput, calls=%fused_computation | convolution fusion | flops 4316987392 | bytes 25190400 | tf_op jit(solution)/shard_map/kt,kd->td/dot_general | solution.py:164
  737.7 6.7 all-gather.17.cloned.1.call-done
  744.3 2.5 reduce_sum.126
  746.9 1.3 convert_element_type.141
  748.2 92.6 %all-reduce.7.cloned.1.call-done = (bf16[128,1024]{1,0:T(8,128)(2,1)}, bf16[128,4096]{1,0:T(8,128)(2,1)}, bf16[512,1024]{1,0:T(8,128)(2,1)}) async-done(((bf16[128,1024]{1,0:T(8,128)(2,1)}, bf16[128,4096]{1,0:T(8,128)(2,1)}, bf16[512,1024]{1,0:T(8,128)(2,1)}), (bf16[128,1024]{1,0:T(8,128)(2,1)}, bf16[128,4096]{1,0:T(8,128)(2,1)}, bf16[512,1024]{1,0:T(8,128)(2,1)})) %all-reduce.7.cloned.1.call-update) | async-done | bytes 2359312 | tf_op jit(solution)/shard_map/psum | solution.py:179
  840.7 1.8 convert_element_type.143
  842.5 2.8 convert_element_type.145
  845.3 2.8 convert_element_type.147
  (68 shorter events, 2.6 us)
Async XLA Ops:
  7.2 50.9 %all-gather.9.cloned.1.call-start = ((), (), s32[]{:S(2)}) async-start(), calls=%async_computation.4 | async-start | bytes 7077888 | tf_op jit(solution)/shard_map/all_gather | solution.py:53
  7.9 92.5 %all-gather.11.cloned.1.call-start = ((), (), s32[]{:S(2)}) async-start(), calls=%async_computation.5 | async-start | bytes 2359296 | tf_op jit(solution)/shard_map/all_gather | solution.py:54
  8.7 135.3 %all-gather.13.cloned.1.call-start = ((), (), s32[]{:S(2)}) async-start(), calls=%async_computation.6 | async-start | bytes 9437184 | tf_op jit(solution)/shard_map/all_gather | solution.py:59
  9.4 190.6 %all-gather.15.cloned.1.call-start = ((), (), s32[]{:S(2)}) async-start(), calls=%async_computation.7 | async-start | bytes 9437184 | tf_op jit(solution)/shard_map/all_gather | solution.py:60
  10.0 374.4 %reduce-scatter.5.cloned.1.call-start = ((), (), s32[]{:S(2)}) async-start(), calls=%async_computation.8 | async-start | bytes 14155776 | tf_op jit(solution)/shard_map/reduce_scatter | solution.py:173
  31.6 7.8 copy-start.10
  39.4 0.7 copy-start.13
  200.0 14.6 %copy-start.1 = (f32[512,1024]{1,0:T(8,128)S(1)}, f32[512,1024]{1,0:T(8,128)}, u32[]{:S(2)}) copy-start(f32[512,1024]{1,0:T(8,128)} %get-tuple-element.21) | copy-start | bytes 6291460
  214.6 10.9 %copy-start.2 = (f32[512,1024]{1,0:T(8,128)S(1)}, f32[512,1024]{1,0:T(8,128)}, u32[]{:S(2)}) copy-start(f32[512,1024]{1,0:T(8,128)} %get-tuple-element.31) | copy-start | bytes 6291460
  214.6 10.9 %copy-start.15 = (bf16[4096,1024]{1,0:T(8,128)(2,1)S(1)}, bf16[4096,1024]{1,0:T(8,128)(2,1)}, u32[]{:S(2)}) copy-start(bf16[4096,1024]{1,0:T(8,128)(2,1)} %all-gather.15.cloned.1.call-done) | copy-start | bytes 25165828
  214.6 10.9 %copy-start.19 = (f32[512,1024]{1,0:T(8,128)S(1)}, f32[512,1024]{1,0:T(8,128)}, u32[]{:S(2)}) copy-start(f32[512,1024]{1,0:T(8,128)} %fusion.12) | copy-start | bytes 6291460
  225.5 11.1 %copy-start.6 = (bf16[1024,1024]{1,0:T(8,128)(2,1)S(1)}, bf16[1024,1024]{1,0:T(8,128)(2,1)}, u32[]{:S(2)}) copy-start(bf16[1024,1024]{1,0:T(8,128)(2,1)} %all-gather.11.cloned.1.call-done) | copy-start | bytes 6291460
  235.7 1.0 copy-start.18
  241.2 10.6 %copy-start.8 = (bf16[512,1024]{0,1:T(8,128)(2,1)S(1)}, bf16[512,1024]{0,1:T(8,128)(2,1)}, u32[]{:S(2)}) copy-start(bf16[512,1024]{0,1:T(8,128)(2,1)} %copy.48) | copy-start | bytes 3145732
  241.2 10.6 %copy-start.9 = (bf16[512,1024]{0,1:T(8,128)(2,1)S(1)}, bf16[512,1024]{0,1:T(8,128)(2,1)}, u32[]{:S(2)}) copy-start(bf16[512,1024]{0,1:T(8,128)(2,1)} %copy.52) | copy-start | bytes 3145732
  251.8 29.4 %copy-start.16 = (bf16[16,64,512]{2,1,0:T(8,128)(2,1)}, bf16[16,64,512]{2,1,0:T(8,128)(2,1)S(1)}, u32[]{:S(2)}) copy-start(bf16[16,64,512]{2,1,0:T(8,128)(2,1)S(1)} %fusion.24) | copy-start | bytes 3145732
  264.6 12.4 %copy-start = (bf16[512,1024]{0,1:T(8,128)(2,1)S(1)}, bf16[512,1024]{0,1:T(8,128)(2,1)}, u32[]{:S(2)}) copy-start(bf16[512,1024]{0,1:T(8,128)(2,1)} %copy.49) | copy-start | bytes 3145732
  279.7 1.5 copy-start.7
  281.1 1.0 copy-start.3
  292.0 1.2 copy-start.5
  292.0 146.8 %reduce-scatter.7.cloned.1.call-start = ((), (), s32[]{:S(2)}) async-start(), calls=%async_computation.9 | async-start | bytes 4718592 | tf_op jit(solution)/shard_map/reduce_scatter | solution.py:174
  297.7 260.9 %reduce-scatter.11.cloned.1.call-start = ((), (), s32[]{:S(2)}) async-start(), calls=%async_computation.11 | async-start | bytes 18874368 | tf_op jit(solution)/shard_map/reduce_scatter | solution.py:169
  315.6 362.8 %reduce-scatter.9.cloned.1.call-start = ((), (), s32[]{:S(2)}) async-start(), calls=%async_computation.10 | async-start | bytes 18874368 | tf_op jit(solution)/shard_map/reduce_scatter | solution.py:168
  329.2 57.7 %copy-start.12 = (bf16[1024]{0:T(1024)(128)(2,1)S(1)}, bf16[1024]{0:T(1024)(128)(2,1)}, u32[]{:S(2)}) copy-start(bf16[1024]{0:T(1024)(128)(2,1)} %param.21) | copy-start | bytes 6148
  329.2 57.7 %copy-start.17 = (u32[32]{0:T(128)S(1)}, u32[32]{0:T(128)}, u32[]{:S(2)}) copy-start(u32[32]{0:T(128)} %constant.41) | copy-start | bytes 388
  329.2 59.0 %copy-start.4 = (bf16[16,64,512]{2,1,0:T(8,128)(2,1)S(1)}, bf16[16,64,512]{2,1,0:T(8,128)(2,1)}, u32[]{:S(2)}) copy-start(bf16[16,64,512]{2,1,0:T(8,128)(2,1)} %copy-done.3) | copy-start | bytes 3145732
  329.2 415.1 %all-gather.17.cloned.1.call-start = ((), (), s32[]{:S(2)}) async-start(), calls=%async_computation.12 | async-start | bytes 3932160 | tf_op jit(solution)/shard_map/all_gather | solution.py:11
  386.8 453.9 %all-reduce.7.cloned.1.call-start = ((), (), s32[]{:S(2)}) async-start(), calls=%async_computation.13 | async-start | bytes 4718592 | tf_op jit(solution)/shard_map/psum | solution.py:179
  388.2 34.3 %copy-start.11 = (s32[512]{0:T(512)S(1)}, s32[512]{0:T(512)}, u32[]{:S(2)}) copy-start(s32[512]{0:T(512)} %param.14) | copy-start | bytes 6148
  432.4 292.7 %copy-start.14 = (f32[512]{0:T(512)S(1)}, f32[512]{0:T(512)}, u32[]{:S(2)}) copy-start(f32[512]{0:T(512)} %copy-done.13) | copy-start | bytes 6148
Sparse Core Ops, SparseCore 0:
  9.9 48.1 all-gather.8
  59.9 27.7 all-gather.10
  89.6 54.2 all-gather.12
  145.7 54.2 all-gather.14
  292.1 92.2 reduce-scatter.4
  387.6 51.1 reduce-scatter.6
  442.4 116.1 reduce-scatter.10
  562.2 116.1 reduce-scatter.8
  679.9 64.3 all-gather.16
  747.3 93.3 all-reduce.6
